TPU v7x, 512 devices: a whole 4x8x8 slice. The times are simulated.
512 devices in a mesh: brick: 128 (over z, y, core), span: 4 (over x).
Axes of the slice: x: 4, y: 8, z: 8, core: 2. Of those that a mesh axis runs over, the one named last changes fastest.
Arguments:
- state: float32 [5, 128, 64, 1024], P(None, 'brick', 'span'), may hold values from -6 to 6
- jacobian_i: float32 [5, 5], replicated, may hold values from -2.5 to 2.5
- jacobian_j: float32 [5, 5], replicated, may hold values from -2.5 to 2.5
- brick_cols: int32 [128], P('brick'), may hold values from 1 to 1024, 81920 in all
- fringe_peer: int32 [128, 4, 2048], P('brick', 'span'), may hold values from 0 to 127, as said below
- fringe_donor: int32 [128, 4, 2048], P('brick', 'span'), may hold values from 0 to 15358, as said below
- fringe_target: int32 [128, 4, 2048], P('brick', 'span'), may hold values from 0 to 16383
- fringe_frac: float32 [2, 128, 4, 2048], P(None, 'brick', 'span'), may hold values from 0 to 1
- wall_patch: int32 [128, 4, 1024], P('brick', 'span'), may hold values from 0 to 16
- wall_angle: float32 [128, 4, 1024], P('brick', 'span'), may hold values from -3.140625 to 3.140625
Outputs:
- state_next: float32 [5, 128, 64, 1024], P(None, 'brick', 'span')
- loads: float32 [3, 16], replicated
Inputs may be any that keep to these rules, and one draw needn't show every extreme that they name: `fringe_peer`: each device sends at most 32 rows to one brick index and exactly 32 to some; receptor targets are distinct on every receiving device. `fringe_donor`: i < 15 and j < 1023 for each donor corner.
All inputs are finite; a program needn't handle non-finite values. No bound on the sum of `brick_cols` on one device may be relied on, other than what follows from the above.
Results may differ from a plain program's by a relative error of at most 0.000071.
Values sent between devices are 32-bit elements; how exact they have to be, the bound alone decides.
No kernel may reach another device: no remote copies, remote signals or barrier semaphores. Data moves between devices by JAX's collectives and lax.ppermute only.
A program may use at most 128 MiB of HBM per device.

v0:
```python
import jax
import jax.numpy as jnp
from jax import lax
from jax.sharding import PartitionSpec as P

NP = 16

viscosity = 0.1
time_step = 0.3

F32 = jnp.float32
BF16 = jnp.bfloat16


def with_halo(block, axis, dim, width):
    count = lax.axis_size(axis)
    forward = [(i, i + 1) for i in range(count - 1)]
    backward = [(target, source) for source, target in forward]
    low = lax.ppermute(
        lax.slice_in_dim(block, block.shape[dim] - width, None, axis=dim), axis, forward
    )
    high = lax.ppermute(lax.slice_in_dim(block, 0, width, axis=dim), axis, backward)
    return jnp.concatenate([low, block, high], axis=dim)


def shift_cols(field, forward):
    zero_col = jnp.zeros(field.shape[:-1] + (1,), field.dtype)
    if forward:
        return jnp.concatenate([field[..., 1:], zero_col], axis=-1)
    return jnp.concatenate([zero_col, field[..., :-1]], axis=-1)


def split_parts(x):
    hi = lax.reduce_precision(x, exponent_bits=8, mantissa_bits=7)
    lo = x - hi
    return jnp.stack([hi, lo]).astype(BF16)


def join_parts(parts):
    return parts[0] + parts[1]


def shards(
    state,
    jacobian_i,
    jacobian_j,
    brick_cols,
    fringe_peer,
    fringe_donor,
    fringe_target,
    fringe_frac,
    wall_patch,
    wall_angle,
):
    var_count = state.shape[0]
    row_count = state.shape[2]
    col_count = state.shape[3]
    peer_count = lax.axis_size("brick")
    fringe_rows = fringe_peer.shape[-1]
    capacity = 2 * fringe_rows // peer_count

    dest_peer = fringe_peer.reshape(fringe_rows)
    donor_cell = fringe_donor.reshape(fringe_rows)
    target_cell = fringe_target.reshape(fringe_rows)
    frac_a = fringe_frac[0].reshape(fringe_rows)
    frac_c = fringe_frac[1].reshape(fringe_rows)

    peer_hot = dest_peer[:, None] == jnp.arange(peer_count, dtype=jnp.int32)[None, :]
    peer_int = peer_hot.astype(jnp.int32)
    rank_in = jnp.sum(jnp.cumsum(peer_int, axis=0) * peer_int, axis=1) - 1
    peer_mat = peer_hot.astype(BF16)
    rank_hot = jnp.arange(capacity, dtype=jnp.int32)[:, None] == rank_in[None, :]

    donor_i = donor_cell // col_count
    donor_j = donor_cell % col_count
    col_mat = (jnp.arange(col_count, dtype=jnp.int32)[:, None] == donor_j[None, :]).astype(BF16)
    row_iota = jnp.arange(row_count, dtype=jnp.int32)[:, None]
    row_lo = row_iota == donor_i[None, :]
    row_hi = row_iota == donor_i[None, :] + 1

    def interpolate(field):
        shifted = jnp.concatenate([field[..., 1:], field[..., :1]], axis=-1)
        pieces = split_parts(jnp.stack([field, shifted]))
        picked = lax.dot_general(
            pieces, col_mat, (((4,), (0,)), ((), ())), preferred_element_type=F32
        )
        picked = join_parts(picked)
        at_lo = jnp.sum(jnp.where(row_lo[None, None], picked, 0.0), axis=2)
        at_hi = jnp.sum(jnp.where(row_hi[None, None], picked, 0.0), axis=2)
        q00, q01 = at_lo[0], at_lo[1]
        q10, q11 = at_hi[0], at_hi[1]
        a = frac_a[None]
        c = frac_c[None]
        interp = (1.0 - a) * (1.0 - c) * q00 + a * (1.0 - c) * q10
        return interp + (1.0 - a) * c * q01 + a * c * q11

    def exchange(values):
        pieces = split_parts(values)
        spread = jnp.where(rank_hot[None, None], pieces[:, :, None, :], jnp.zeros((), BF16))
        packed = lax.dot_general(
            peer_mat, spread, (((0,), (3,)), ((), ())), preferred_element_type=F32
        )
        packed = packed[:, 0] + packed[:, 1]
        flat = packed.reshape(peer_count, 1, packed.shape[1] * packed.shape[2])
        moved = lax.all_to_all(flat, "brick", 0, 0, tiled=True)
        return moved.reshape(packed.shape)

    local_state = state[:, 0]

    first_interp = interpolate(local_state)
    target_code = (target_cell + 1).astype(F32)
    received = exchange(jnp.concatenate([first_interp, target_code[None]], axis=0))
    slot_count = peer_count * capacity

    def flat_slots(values):
        return jnp.transpose(values, (1, 0, 2)).reshape(values.shape[1], slot_count)

    recv_cells = flat_slots(received[:, var_count:]).astype(jnp.int32)[0] - 1
    recv_i = jnp.floor_divide(recv_cells, col_count)
    recv_j = recv_cells - recv_i * col_count
    cell_mat = (
        recv_j[:, None] == jnp.arange(col_count, dtype=jnp.int32)[None, :]
    ).astype(BF16)
    recv_row = jnp.arange(row_count, dtype=jnp.int32)[:, None] == recv_i[None]

    def spread_values(values):
        pieces = split_parts(flat_slots(values))
        return jnp.where(recv_row[None, None], pieces[:, :, None], jnp.zeros((), BF16))

    def to_cells(spread):
        return lax.dot_general(
            spread, cell_mat, (((3,), (0,)), ((), ())), preferred_element_type=F32
        )

    first_spread = spread_values(received[:, :var_count])
    marks = jnp.broadcast_to(recv_row.astype(BF16)[None, None], (2, 1) + recv_row.shape)
    first_cells = to_cells(jnp.concatenate([first_spread, marks], axis=1))
    hit = first_cells[0, var_count] > 0.5

    def place(field, values, cells=None):
        if cells is None:
            cells = to_cells(spread_values(values))
        placed = join_parts(cells)
        return jnp.where(hit[None], placed, field)

    def fringe(field):
        return place(field, exchange(interpolate(field)))

    live_mask = (jnp.arange(col_count, dtype=jnp.int32) < brick_cols[0]).astype(F32)[None, None, :]

    def rhs(field):
        extended = with_halo(field, "span", 1, 1)
        upper = extended[:, 2:, :]
        lower = extended[:, :-2, :]
        right = shift_cols(field, True)
        left = shift_cols(field, False)
        diff_i = upper - lower
        diff_j = right - left
        laplace = upper + lower + right + left - 4.0 * field
        advect = sum(
            jacobian_i[:, w, None, None] * diff_i[w] + jacobian_j[:, w, None, None] * diff_j[w]
            for w in range(field.shape[0])
        )
        return (-0.5 * advect + viscosity * laplace) * live_mask

    section_zero = place(local_state, None, first_cells[:, :var_count])
    section_one = fringe(section_zero + time_step * rhs(section_zero))
    section_two = fringe(0.75 * section_zero + 0.25 * (section_one + time_step * rhs(section_one)))
    state_next = section_zero / 3.0 + 2.0 / 3.0 * (section_two + time_step * rhs(section_two))
    span_count = lax.axis_size("span")
    wall_dir = wall_angle.reshape(col_count)
    own_geom = jnp.stack(
        [(wall_patch.reshape(col_count) + 1).astype(F32), jnp.cos(wall_dir), jnp.sin(wall_dir)]
    )
    next_geom = lax.ppermute(own_geom, "span", [(i + 1, i) for i in range(span_count - 1)])
    xpos = (jnp.arange(col_count, dtype=F32) + 0.5) / col_count - 0.5
    live_row = live_mask[0, 0]

    def wall_partial(pressure, geom):
        patch = geom[0].astype(jnp.int32) - 1
        patch_hot = (patch[:, None] == jnp.arange(NP, dtype=jnp.int32)[None, :]).astype(F32)
        force_x = pressure * geom[1]
        force_y = pressure * geom[2]
        contrib = jnp.stack([force_x, force_y, xpos * force_y])
        return jnp.dot(contrib, patch_hot, precision=lax.Precision.HIGHEST)

    first = section_two[:, 0]
    diff_j = shift_cols(first, True) - shift_cols(first, False)
    laplace = section_two[4, 1] + shift_cols(first[4], True) + shift_cols(first[4], False)
    laplace = laplace - 4.0 * first[4]
    advect = jnp.dot(jacobian_i[4], section_two[:, 1], precision=lax.Precision.HIGHEST)
    advect = advect + jnp.dot(jacobian_j[4], diff_j, precision=lax.Precision.HIGHEST)
    own_rate = (-0.5 * advect + viscosity * laplace) * live_row
    own_pressure = section_zero[4, 0] / 3.0 + 2.0 / 3.0 * (first[4] + time_step * own_rate)
    last = section_two[:, -1]
    halo_rate = (0.5 * jnp.dot(jacobian_i[4], last, precision=lax.Precision.HIGHEST) + viscosity * last[4]) * live_row
    next_pressure = 2.0 / 3.0 * (time_step * halo_rate)
    partial_loads = wall_partial(own_pressure, own_geom) + wall_partial(next_pressure, next_geom)
    span_loads = lax.psum(partial_loads, "span")
    copies = jnp.broadcast_to(span_loads[None], (peer_count,) + span_loads.shape)
    gathered = lax.all_to_all(copies, "brick", 0, 0, tiled=True)
    loads = jnp.sum(gathered, axis=0) / col_count
    return (state_next[:, None], loads)


def solution(mesh):
    return jax.shard_map(
        shards,
        mesh=mesh,
        in_specs=(
            P(None, "brick", "span", None),
            P(),
            P(),
            P("brick"),
            P("brick", "span", None),
            P("brick", "span", None),
            P("brick", "span", None),
            P(None, "brick", "span", None),
            P("brick", "span", None),
            P("brick", "span", None),
        ),
        out_specs=(P(None, "brick", "span", None), P()),
        check_vma=False,
    )
```

profile of v0, /device:TPU:1, one launch (start us, length us, event | category | flops | bytes accessed | tf_op | source)
XLA Modules:
  0.0 159.0 jit_solution(870049722955331502)
XLA Ops:
  7.6 1.9 %fusion.15 = f32[2,2,5,16,2048]{4,3,2,1,0:T(8,128)S(1)} fusion(s32[2048]{0:T(1024)S(1)} %get-tuple-element.119, bf16[1,2,5,16,1024]{4,3,2,1,0:T(8,128)(2,1)S(1)} %get-tuple-element.62, bf16[1,2,5,16,1024]{4,3,2,1,0:T(8,128)(2,1)S(1)} %get-tuple-element.61), kind=kOutput, calls=%fused_computation.12 | convolution fusion | flops 1344602112 | bytes 3284992 | tf_op jit(solution)/shard_map/dot_general | solution.py:84
  11.7 18.4 %all-to-all-start = ((f32[128,1,192]{2,1,0:T(1,128)}), f32[128,1,192]{2,1,0:T(1,128)S(1)}, u32[]{:S(2)}, u32[]{:S(2)}) async-start(f32[128,1,192]{2,1,0:T(1,128)} %copy.55), calls=%async_computation | async-start | bytes 262144 | tf_op jit(solution)/shard_map/all_to_all | solution.py:105
  30.3 1.3 collective-permute-start.6
  32.6 2.5 %collective-permute-done.6 = f32[3,1024]{1,0:T(4,128)S(1)} collective-permute-done((f32[3,1024]{1,0:T(4,128)S(1)}, f32[3,1024]{1,0:T(4,128)S(1)}, u32[]{:S(2)}, u32[]{:S(2)}) %collective-permute-start.6) | collective-permute-done | bytes 12320 | tf_op jit(solution)/shard_map/ppermute | solution.py:175
  35.1 7.7 %all-to-all-done = f32[128,1,192]{2,1,0:T(1,128)S(1)} async-done(((f32[128,1,192]{2,1,0:T(1,128)}), f32[128,1,192]{2,1,0:T(1,128)S(1)}, u32[]{:S(2)}, u32[]{:S(2)}) %all-to-all-start) | async-done | bytes 98336 | tf_op jit(solution)/shard_map/all_to_all | solution.py:105
  43.8 3.6 %fusion.5 = f32[2,6,16,1024]{3,2,1,0:T(8,128)S(1)} fusion(s32[4096]{0:T(1024)S(1)} %get-tuple-element.111, bf16[2,1,16,4096]{3,2,1,0:T(8,128)(2,1)S(1)} %broadcast_in_dim.198, bf16[2,5,16,4096]{3,2,1,0:T(8,128)(2,1)S(1)} %broadcast_select_fusion), kind=kOutput, calls=%fused_computation.4 | convolution fusion | flops 1615593472 | bytes 2375680 | tf_op jit(solution)/shard_map/dot_general | solution.py:131
  47.7 1.3 collective-permute-start
  49.0 4.2 %collective-permute-start.1 = (f32[5,1,1024]{2,1,0:T(1,128)S(1)}, f32[5,1,1024]{2,1,0:T(1,128)S(1)}, u32[]{:S(2)}, u32[]{:S(2)}) collective-permute-start(f32[5,1,1024]{2,1,0:T(1,128)S(1)} %get-tuple-element.94), channel_id=1, source_target_pairs={{0,1},{1,2},{2,3},{4,5},{5,6},{6,7},{8,9},{9,10},{10,11},{12,13},{... | collective-permute-start | bytes 61448 | tf_op jit(solution)/shard_map/ppermute | solution.py:19
  54.9 1.9 %fusion.13 = f32[2,2,5,16,2048]{4,3,2,1,0:T(8,128)S(1)} fusion(s32[2048]{0:T(1024)S(1)} %get-tuple-element.119, bf16[1,2,5,16,1024]{4,3,2,1,0:T(8,128)(2,1)S(1)} %get-tuple-element.55, bf16[1,2,5,16,1024]{4,3,2,1,0:T(8,128)(2,1)S(1)} %get-tuple-element.54), kind=kOutput, calls=%fused_computation.11 | convolution fusion | flops 1344602112 | bytes 3284992 | tf_op jit(solution)/shard_map/dot_general | solution.py:84
  58.9 8.0 %all-to-all-start.1 = ((f32[128,1,160]{2,1,0:T(1,128)}), f32[128,1,160]{2,1,0:T(1,128)S(1)}, u32[]{:S(2)}, u32[]{:S(2)}) async-start(f32[128,1,160]{2,1,0:T(1,128)} %copy.59), calls=%async_computation.1 | async-start | bytes 262144 | tf_op jit(solution)/shard_map/all_to_all | solution.py:105
  66.9 12.7 %all-to-all-done.1 = f32[128,1,160]{2,1,0:T(1,128)S(1)} async-done(((f32[128,1,160]{2,1,0:T(1,128)}), f32[128,1,160]{2,1,0:T(1,128)S(1)}, u32[]{:S(2)}, u32[]{:S(2)}) %all-to-all-start.1) | async-done | bytes 81952 | tf_op jit(solution)/shard_map/all_to_all | solution.py:105
  80.1 3.4 %fusion.3 = f32[2,5,16,1024]{3,2,1,0:T(8,128)S(1)} fusion(s32[4096]{0:T(1024)S(1)} %get-tuple-element.111, pred[16,4096]{1,0:T(8,128)(4,1)S(1)} %get-tuple-element.108, bf16[2,5,4096]{2,1,0:T(8,128)(2,1)S(1)} %pad_maximum_fusion.10), kind=kOutput, calls=%fused_computation.3 | convolution fusion | flops 1347026944 | bytes 819200 | tf_op jit(solution)/shard_map/dot_general | solution.py:131
  83.8 1.3 collective-permute-start.2
  85.1 4.8 %collective-permute-start.3 = (f32[5,1,1024]{2,1,0:T(1,128)S(1)}, f32[5,1,1024]{2,1,0:T(1,128)S(1)}, u32[]{:S(2)}, u32[]{:S(2)}) collective-permute-start(f32[5,1,1024]{2,1,0:T(1,128)S(1)} %get-tuple-element.85), channel_id=1, source_target_pairs={{0,1},{1,2},{2,3},{4,5},{5,6},{6,7},{8,9},{9,10},{10,11},{12,13},{... | collective-permute-start | bytes 61448 | tf_op jit(solution)/shard_map/ppermute | solution.py:19
  91.6 1.9 %fusion.11 = f32[2,2,5,16,2048]{4,3,2,1,0:T(8,128)S(1)} fusion(s32[2048]{0:T(1024)S(1)} %get-tuple-element.119, bf16[1,2,5,16,1024]{4,3,2,1,0:T(8,128)(2,1)S(1)} %get-tuple-element.48, bf16[1,2,5,16,1024]{4,3,2,1,0:T(8,128)(2,1)S(1)} %get-tuple-element.47), kind=kOutput, calls=%fused_computation.10 | convolution fusion | flops 1344602112 | bytes 3284992 | tf_op jit(solution)/shard_map/dot_general | solution.py:84
  95.6 6.4 %all-to-all-start.2 = ((f32[128,1,160]{2,1,0:T(1,128)}), f32[128,1,160]{2,1,0:T(1,128)S(1)}, u32[]{:S(2)}, u32[]{:S(2)}) async-start(f32[128,1,160]{2,1,0:T(1,128)} %copy.62), calls=%async_computation.2 | async-start | bytes 262144 | tf_op jit(solution)/shard_map/all_to_all | solution.py:105
  102.0 12.8 %all-to-all-done.2 = f32[128,1,160]{2,1,0:T(1,128)S(1)} async-done(((f32[128,1,160]{2,1,0:T(1,128)}), f32[128,1,160]{2,1,0:T(1,128)S(1)}, u32[]{:S(2)}, u32[]{:S(2)}) %all-to-all-start.2) | async-done | bytes 81952 | tf_op jit(solution)/shard_map/all_to_all | solution.py:105
  115.3 3.4 %fusion.1 = f32[2,5,16,1024]{3,2,1,0:T(8,128)S(1)} fusion(s32[4096]{0:T(1024)S(1)} %get-tuple-element.111, pred[16,4096]{1,0:T(8,128)(4,1)S(1)} %get-tuple-element.108, bf16[2,5,4096]{2,1,0:T(8,128)(2,1)S(1)} %pad_maximum_fusion.11), kind=kOutput, calls=%fused_computation.2 | convolution fusion | flops 1347026944 | bytes 819200 | tf_op jit(solution)/shard_map/dot_general | solution.py:131
  119.0 1.3 collective-permute-start.4
  120.5 4.6 %collective-permute-start.5 = (f32[5,1,1024]{2,1,0:T(1,128)S(1)}, f32[5,1,1024]{2,1,0:T(1,128)S(1)}, u32[]{:S(2)}, u32[]{:S(2)}) collective-permute-start(f32[5,1,1024]{2,1,0:T(1,128)S(1)} %get-tuple-element.67), channel_id=1, source_target_pairs={{0,1},{1,2},{2,3},{4,5},{5,6},{6,7},{8,9},{9,10},{10,11},{12,13},{... | collective-permute-start | bytes 61448 | tf_op jit(solution)/shard_map/ppermute | solution.py:19
  126.6 7.8 %psum.7 = f32[3,16]{1,0:T(4,128)S(1)} all-reduce(f32[3,16]{1,0:T(4,128)S(1)} %convolution_add_fusion), channel_id=1, replica_groups=mesh['brick'=128,'span'=4] {'span'}, use_global_device_ids=true, to_apply=%region_9.10 | all-reduce | flops 48 | bytes 384 | tf_op jit(solution)/shard_map/psum | solution.py:199
  135.1 7.8 %all-to-all-start.3 = ((f32[128,3,16]{2,1,0:T(4,128)}), f32[128,3,16]{2,1,0:T(4,128)S(1)}, u32[]{:S(2)}, u32[]{:S(2)}) async-start(f32[128,3,16]{2,1,0:T(4,128)} %broadcast_in_dim.207), calls=%async_computation.3 | async-start | bytes 524288 | tf_op jit(solution)/shard_map/all_to_all | solution.py:201
  143.2 1.3 add_bitcast_fusion
  144.5 13.8 %all-to-all-done.3 = f32[128,3,16]{2,1,0:T(4,128)S(1)} async-done(((f32[128,3,16]{2,1,0:T(4,128)}), f32[128,3,16]{2,1,0:T(4,128)S(1)}, u32[]{:S(2)}, u32[]{:S(2)}) %all-to-all-start.3) | async-done | bytes 24608 | tf_op jit(solution)/shard_map/all_to_all | solution.py:201
  (133 shorter events, 22.8 us)
Async XLA Ops:
  5.9 0.7 copy-start.3
  6.0 1.5 copy-start
  10.2 20.0 %copy-start.4 = (f32[1,1,1024]{2,1,0:T(1,128)S(1)}, f32[1,1,1024]{2,1,0:T(1,128)}, u32[]{:S(2)}) copy-start(f32[1,1,1024]{2,1,0:T(1,128)} %param.19) | copy-start | bytes 12292
  10.2 20.1 %copy-start.5 = (s32[1,1,1024]{2,1,0:T(1,128)S(1)}, s32[1,1,1024]{2,1,0:T(1,128)}, u32[]{:S(2)}) copy-start(s32[1,1,1024]{2,1,0:T(1,128)} %param.18) | copy-start | bytes 12292
  10.2 22.1 %copy-start.1 = (f32[5,5]{1,0:T(8,128)S(1)}, f32[5,5]{1,0:T(8,128)}, u32[]{:S(2)}) copy-start(f32[5,5]{1,0:T(8,128)} %param.11) | copy-start | bytes 304
  10.2 22.1 %copy-start.2 = (f32[5,5]{1,0:T(8,128)S(1)}, f32[5,5]{1,0:T(8,128)}, u32[]{:S(2)}) copy-start(f32[5,5]{1,0:T(8,128)} %param.12) | copy-start | bytes 304
  11.7 31.2 %all-to-all-start = ((f32[128,1,192]{2,1,0:T(1,128)}), f32[128,1,192]{2,1,0:T(1,128)S(1)}, u32[]{:S(2)}, u32[]{:S(2)}) async-start(f32[128,1,192]{2,1,0:T(1,128)} %copy.55), calls=%async_computation | async-start | bytes 262144 | tf_op jit(solution)/shard_map/all_to_all | solution.py:105
  30.3 4.8 %collective-permute-start.6 = (f32[3,1024]{1,0:T(4,128)S(1)}, f32[3,1024]{1,0:T(4,128)S(1)}, u32[]{:S(2)}, u32[]{:S(2)}) collective-permute-start(f32[3,1024]{1,0:T(4,128)S(1)} %pad_maximum_fusion.16), channel_id=1, source_target_pairs={{1,0},{2,1},{3,2},{5,4},{6,5},{7,6},{9,8},{10,9},{11,10},{13,12},{... | collective-permute-start | bytes 36872 | tf_op jit(solution)/shard_map/ppermute | solution.py:175
  47.7 5.6 %collective-permute-start = (f32[5,1,1024]{2,1,0:T(1,128)S(1)}, f32[5,1,1024]{2,1,0:T(1,128)S(1)}, u32[]{:S(2)}, u32[]{:S(2)}) collective-permute-start(f32[5,1,1024]{2,1,0:T(1,128)S(1)} %get-tuple-element.95), channel_id=1, source_target_pairs={{1,0},{2,1},{3,2},{5,4},{6,5},{7,6},{9,8},{10,9},{11,10},{13,12},{... | collective-permute-start | bytes 61448 | tf_op jit(solution)/shard_map/ppermute | solution.py:22
  49.0 4.9 %collective-permute-start.1 = (f32[5,1,1024]{2,1,0:T(1,128)S(1)}, f32[5,1,1024]{2,1,0:T(1,128)S(1)}, u32[]{:S(2)}, u32[]{:S(2)}) collective-permute-start(f32[5,1,1024]{2,1,0:T(1,128)S(1)} %get-tuple-element.94), channel_id=1, source_target_pairs={{0,1},{1,2},{2,3},{4,5},{5,6},{6,7},{8,9},{9,10},{10,11},{12,13},{... | collective-permute-start | bytes 61448 | tf_op jit(solution)/shard_map/ppermute | solution.py:19
  58.9 20.7 %all-to-all-start.1 = ((f32[128,1,160]{2,1,0:T(1,128)}), f32[128,1,160]{2,1,0:T(1,128)S(1)}, u32[]{:S(2)}, u32[]{:S(2)}) async-start(f32[128,1,160]{2,1,0:T(1,128)} %copy.59), calls=%async_computation.1 | async-start | bytes 262144 | tf_op jit(solution)/shard_map/all_to_all | solution.py:105
  83.8 6.2 %collective-permute-start.2 = (f32[5,1,1024]{2,1,0:T(1,128)S(1)}, f32[5,1,1024]{2,1,0:T(1,128)S(1)}, u32[]{:S(2)}, u32[]{:S(2)}) collective-permute-start(f32[5,1,1024]{2,1,0:T(1,128)S(1)} %get-tuple-element.86), channel_id=1, source_target_pairs={{1,0},{2,1},{3,2},{5,4},{6,5},{7,6},{9,8},{10,9},{11,10},{13,12},{... | collective-permute-start | bytes 61448 | tf_op jit(solution)/shard_map/ppermute | solution.py:22
  85.1 5.4 %collective-permute-start.3 = (f32[5,1,1024]{2,1,0:T(1,128)S(1)}, f32[5,1,1024]{2,1,0:T(1,128)S(1)}, u32[]{:S(2)}, u32[]{:S(2)}) collective-permute-start(f32[5,1,1024]{2,1,0:T(1,128)S(1)} %get-tuple-element.85), channel_id=1, source_target_pairs={{0,1},{1,2},{2,3},{4,5},{5,6},{6,7},{8,9},{9,10},{10,11},{12,13},{... | collective-permute-start | bytes 61448 | tf_op jit(solution)/shard_map/ppermute | solution.py:19
  95.6 19.3 %all-to-all-start.2 = ((f32[128,1,160]{2,1,0:T(1,128)}), f32[128,1,160]{2,1,0:T(1,128)S(1)}, u32[]{:S(2)}, u32[]{:S(2)}) async-start(f32[128,1,160]{2,1,0:T(1,128)} %copy.62), calls=%async_computation.2 | async-start | bytes 262144 | tf_op jit(solution)/shard_map/all_to_all | solution.py:105
  119.0 24.1 %collective-permute-start.4 = (f32[5,1,1024]{2,1,0:T(1,128)S(1)}, f32[5,1,1024]{2,1,0:T(1,128)S(1)}, u32[]{:S(2)}, u32[]{:S(2)}) collective-permute-start(f32[5,1,1024]{2,1,0:T(1,128)S(1)} %get-tuple-element.68), channel_id=1, source_target_pairs={{1,0},{2,1},{3,2},{5,4},{6,5},{7,6},{9,8},{10,9},{11,10},{13,12},{... | collective-permute-start | bytes 61448 | tf_op jit(solution)/shard_map/ppermute | solution.py:22
  120.5 22.6 %collective-permute-start.5 = (f32[5,1,1024]{2,1,0:T(1,128)S(1)}, f32[5,1,1024]{2,1,0:T(1,128)S(1)}, u32[]{:S(2)}, u32[]{:S(2)}) collective-permute-start(f32[5,1,1024]{2,1,0:T(1,128)S(1)} %get-tuple-element.67), channel_id=1, source_target_pairs={{0,1},{1,2},{2,3},{4,5},{5,6},{6,7},{8,9},{9,10},{10,11},{12,13},{... | collective-permute-start | bytes 61448 | tf_op jit(solution)/shard_map/ppermute | solution.py:19
  135.1 23.1 %all-to-all-start.3 = ((f32[128,3,16]{2,1,0:T(4,128)}), f32[128,3,16]{2,1,0:T(4,128)S(1)}, u32[]{:S(2)}, u32[]{:S(2)}) async-start(f32[128,3,16]{2,1,0:T(4,128)} %broadcast_in_dim.207), calls=%async_computation.3 | async-start | bytes 524288 | tf_op jit(solution)/shard_map/all_to_all | solution.py:201
where the time goes:
time: 160 us; the launch traced here: 159 us
  starting transfers between devices  59.3 us (37%)
  waiting for transfers between devices  50.6 us (32%)
  matrix products  19.4 us (12%)
  local copies, waits for them, and re-layouts  10.2 us (6%)
  other arithmetic  9.66 us (6%)
  blocking collectives  7.83 us (5%)
  between operations  2.08 us (1%)
    all_to_all x3, waiting for transfers between devices, exchange(): moved = lax.all_to_all(flat, 'brick', 0, 0, tiled=True)  33.3 us
    all_to_all x3, starting transfers between devices, exchange(): moved = lax.all_to_all(flat, 'brick', 0, 0, tiled=True)  32.8 us
    all_to_all x1, waiting for transfers between devices, shards(): gathered = lax.all_to_all(copies, 'brick', 0, 0, tiled=True)  13.8 us
    ppermute x3, starting transfers between devices, with_halo(): lax.ppermute(lax.slice_in_dim(block, block.shape[dim] - width, None, axis...  13.5 us
    dot_general x3, matrix products, to_cells(): lax.dot_general(spread, cell_mat, (((3,), (0,)), ((), ())), preferred_ele...  10.4 us
    psum x1, blocking collectives, shards(): span_loads = lax.psum(partial_loads, 'span')  7.83 us
    all_to_all x1, starting transfers between devices, shards(): gathered = lax.all_to_all(copies, 'brick', 0, 0, tiled=True)  7.77 us
    dot_general x3, matrix products, interpolate(): lax.dot_general(pieces, col_mat, (((4,), (0,)), ((), ())), preferred_elem...  5.72 us
  transfers between devices with their start and end apart: 11, of which 7 were waited for; matrix products, arithmetic and copies ran while one was open for 3% of the time, Pallas kernels for 0%

commit v1 on v0

--- a/solution.py
+++ b/solution.py
@@ -197,9 +197,9 @@
     next_pressure = 2.0 / 3.0 * (time_step * halo_rate)
     partial_loads = wall_partial(own_pressure, own_geom) + wall_partial(next_pressure, next_geom)
     span_loads = lax.psum(partial_loads, "span")
-    copies = jnp.broadcast_to(span_loads[None], (peer_count,) + span_loads.shape)
+    copies = jnp.broadcast_to(span_loads.reshape(1, 1, -1), (peer_count, 1, span_loads.size))
     gathered = lax.all_to_all(copies, "brick", 0, 0, tiled=True)
-    loads = jnp.sum(gathered, axis=0) / col_count
+    loads = jnp.sum(gathered, axis=(0, 1)).reshape(span_loads.shape) / col_count
     return (state_next[:, None], loads)
 
 

time: 160 us -> 156 us (0.975)
  waiting for transfers between devices: 50.6 us -> 46.8 us
    all_to_all x1, waiting for transfers between devices: 13.8 us -> 9.97 us  [shards(): gathered = lax.all_to_all(copies, 'brick', 0, 0, tiled=True)]
where the time goes in v1:
time: 156 us; the launch traced here: 155 us
  starting transfers between devices  59.3 us (38%)
  waiting for transfers between devices  46.8 us (30%)
  matrix products  19.4 us (12%)
  local copies, waits for them, and re-layouts  10.9 us (7%)
  other arithmetic  9.09 us (6%)
  blocking collectives  7.81 us (5%)
  between operations  2.08 us (1%)
    all_to_all x3, waiting for transfers between devices, exchange(): moved = lax.all_to_all(flat, 'brick', 0, 0, tiled=True)  33.3 us
    all_to_all x3, starting transfers between devices, exchange(): moved = lax.all_to_all(flat, 'brick', 0, 0, tiled=True)  32.8 us
    ppermute x3, starting transfers between devices, with_halo(): lax.ppermute(lax.slice_in_dim(block, block.shape[dim] - width, None, axis...  13.5 us
    dot_general x3, matrix products, to_cells(): lax.dot_general(spread, cell_mat, (((3,), (0,)), ((), ())), preferred_ele...  10.4 us
    all_to_all x1, waiting for transfers between devices, shards(): gathered = lax.all_to_all(copies, 'brick', 0, 0, tiled=True)  9.97 us
    psum x1, blocking collectives, shards(): span_loads = lax.psum(partial_loads, 'span')  7.81 us
    all_to_all x1, starting transfers between devices, shards(): gathered = lax.all_to_all(copies, 'brick', 0, 0, tiled=True)  7.77 us
    dot_general x3, matrix products, interpolate(): lax.dot_general(pieces, col_mat, (((4,), (0,)), ((), ())), preferred_elem...  5.72 us
  transfers between devices with their start and end apart: 11, of which 7 were waited for; matrix products, arithmetic and copies ran while one was open for 3% of the time, Pallas kernels for 0%

profile of v1, /device:TPU:1, one launch (start us, length us, event | category | flops | bytes accessed | tf_op | source)
XLA Modules:
  0.0 155.3 jit_solution(15783842370994149980)
XLA Ops:
  7.6 1.9 %fusion.15 = f32[2,2,5,16,2048]{4,3,2,1,0:T(8,128)S(1)} fusion(s32[2048]{0:T(1024)S(1)} %get-tuple-element.119, bf16[1,2,5,16,1024]{4,3,2,1,0:T(8,128)(2,1)S(1)} %get-tuple-element.62, bf16[1,2,5,16,1024]{4,3,2,1,0:T(8,128)(2,1)S(1)} %get-tuple-element.61), kind=kOutput, calls=%fused_computation.12 | convolution fusion | flops 1344602112 | bytes 3284992 | tf_op jit(solution)/shard_map/dot_general | solution.py:84
  11.7 18.4 %all-to-all-start = ((f32[128,1,192]{2,1,0:T(1,128)}), f32[128,1,192]{2,1,0:T(1,128)S(1)}, u32[]{:S(2)}, u32[]{:S(2)}) async-start(f32[128,1,192]{2,1,0:T(1,128)} %copy.55), calls=%async_computation | async-start | bytes 262144 | tf_op jit(solution)/shard_map/all_to_all | solution.py:105
  30.3 1.3 collective-permute-start.6
  32.6 2.5 %collective-permute-done.6 = f32[3,1024]{1,0:T(4,128)S(1)} collective-permute-done((f32[3,1024]{1,0:T(4,128)S(1)}, f32[3,1024]{1,0:T(4,128)S(1)}, u32[]{:S(2)}, u32[]{:S(2)}) %collective-permute-start.6) | collective-permute-done | bytes 12320 | tf_op jit(solution)/shard_map/ppermute | solution.py:175
  35.1 7.7 %all-to-all-done = f32[128,1,192]{2,1,0:T(1,128)S(1)} async-done(((f32[128,1,192]{2,1,0:T(1,128)}), f32[128,1,192]{2,1,0:T(1,128)S(1)}, u32[]{:S(2)}, u32[]{:S(2)}) %all-to-all-start) | async-done | bytes 98336 | tf_op jit(solution)/shard_map/all_to_all | solution.py:105
  43.8 3.6 %fusion.5 = f32[2,6,16,1024]{3,2,1,0:T(8,128)S(1)} fusion(s32[4096]{0:T(1024)S(1)} %get-tuple-element.111, bf16[2,1,16,4096]{3,2,1,0:T(8,128)(2,1)S(1)} %broadcast_in_dim.199, bf16[2,5,16,4096]{3,2,1,0:T(8,128)(2,1)S(1)} %broadcast_select_fusion), kind=kOutput, calls=%fused_computation.4 | convolution fusion | flops 1615593472 | bytes 2375680 | tf_op jit(solution)/shard_map/dot_general | solution.py:131
  47.7 1.3 collective-permute-start
  49.0 4.2 %collective-permute-start.1 = (f32[5,1,1024]{2,1,0:T(1,128)S(1)}, f32[5,1,1024]{2,1,0:T(1,128)S(1)}, u32[]{:S(2)}, u32[]{:S(2)}) collective-permute-start(f32[5,1,1024]{2,1,0:T(1,128)S(1)} %get-tuple-element.94), channel_id=1, source_target_pairs={{0,1},{1,2},{2,3},{4,5},{5,6},{6,7},{8,9},{9,10},{10,11},{12,13},{... | collective-permute-start | bytes 61448 | tf_op jit(solution)/shard_map/ppermute | solution.py:19
  54.9 1.9 %fusion.13 = f32[2,2,5,16,2048]{4,3,2,1,0:T(8,128)S(1)} fusion(s32[2048]{0:T(1024)S(1)} %get-tuple-element.119, bf16[1,2,5,16,1024]{4,3,2,1,0:T(8,128)(2,1)S(1)} %get-tuple-element.55, bf16[1,2,5,16,1024]{4,3,2,1,0:T(8,128)(2,1)S(1)} %get-tuple-element.54), kind=kOutput, calls=%fused_computation.11 | convolution fusion | flops 1344602112 | bytes 3284992 | tf_op jit(solution)/shard_map/dot_general | solution.py:84
  58.9 8.0 %all-to-all-start.1 = ((f32[128,1,160]{2,1,0:T(1,128)}), f32[128,1,160]{2,1,0:T(1,128)S(1)}, u32[]{:S(2)}, u32[]{:S(2)}) async-start(f32[128,1,160]{2,1,0:T(1,128)} %copy.59), calls=%async_computation.1 | async-start | bytes 262144 | tf_op jit(solution)/shard_map/all_to_all | solution.py:105
  66.9 12.7 %all-to-all-done.1 = f32[128,1,160]{2,1,0:T(1,128)S(1)} async-done(((f32[128,1,160]{2,1,0:T(1,128)}), f32[128,1,160]{2,1,0:T(1,128)S(1)}, u32[]{:S(2)}, u32[]{:S(2)}) %all-to-all-start.1) | async-done | bytes 81952 | tf_op jit(solution)/shard_map/all_to_all | solution.py:105
  80.1 3.4 %fusion.3 = f32[2,5,16,1024]{3,2,1,0:T(8,128)S(1)} fusion(s32[4096]{0:T(1024)S(1)} %get-tuple-element.111, pred[16,4096]{1,0:T(8,128)(4,1)S(1)} %get-tuple-element.108, bf16[2,5,4096]{2,1,0:T(8,128)(2,1)S(1)} %pad_maximum_fusion.10), kind=kOutput, calls=%fused_computation.3 | convolution fusion | flops 1347026944 | bytes 819200 | tf_op jit(solution)/shard_map/dot_general | solution.py:131
  83.8 1.3 collective-permute-start.2
  85.1 4.8 %collective-permute-start.3 = (f32[5,1,1024]{2,1,0:T(1,128)S(1)}, f32[5,1,1024]{2,1,0:T(1,128)S(1)}, u32[]{:S(2)}, u32[]{:S(2)}) collective-permute-start(f32[5,1,1024]{2,1,0:T(1,128)S(1)} %get-tuple-element.85), channel_id=1, source_target_pairs={{0,1},{1,2},{2,3},{4,5},{5,6},{6,7},{8,9},{9,10},{10,11},{12,13},{... | collective-permute-start | bytes 61448 | tf_op jit(solution)/shard_map/ppermute | solution.py:19
  91.6 1.9 %fusion.11 = f32[2,2,5,16,2048]{4,3,2,1,0:T(8,128)S(1)} fusion(s32[2048]{0:T(1024)S(1)} %get-tuple-element.119, bf16[1,2,5,16,1024]{4,3,2,1,0:T(8,128)(2,1)S(1)} %get-tuple-element.48, bf16[1,2,5,16,1024]{4,3,2,1,0:T(8,128)(2,1)S(1)} %get-tuple-element.47), kind=kOutput, calls=%fused_computation.10 | convolution fusion | flops 1344602112 | bytes 3284992 | tf_op jit(solution)/shard_map/dot_general | solution.py:84
  95.6 6.4 %all-to-all-start.2 = ((f32[128,1,160]{2,1,0:T(1,128)}), f32[128,1,160]{2,1,0:T(1,128)S(1)}, u32[]{:S(2)}, u32[]{:S(2)}) async-start(f32[128,1,160]{2,1,0:T(1,128)} %copy.62), calls=%async_computation.2 | async-start | bytes 262144 | tf_op jit(solution)/shard_map/all_to_all | solution.py:105
  102.0 12.8 %all-to-all-done.2 = f32[128,1,160]{2,1,0:T(1,128)S(1)} async-done(((f32[128,1,160]{2,1,0:T(1,128)}), f32[128,1,160]{2,1,0:T(1,128)S(1)}, u32[]{:S(2)}, u32[]{:S(2)}) %all-to-all-start.2) | async-done | bytes 81952 | tf_op jit(solution)/shard_map/all_to_all | solution.py:105
  115.3 3.4 %fusion.1 = f32[2,5,16,1024]{3,2,1,0:T(8,128)S(1)} fusion(s32[4096]{0:T(1024)S(1)} %get-tuple-element.111, pred[16,4096]{1,0:T(8,128)(4,1)S(1)} %get-tuple-element.108, bf16[2,5,4096]{2,1,0:T(8,128)(2,1)S(1)} %pad_maximum_fusion.11), kind=kOutput, calls=%fused_computation.2 | convolution fusion | flops 1347026944 | bytes 819200 | tf_op jit(solution)/shard_map/dot_general | solution.py:131
  119.0 1.3 collective-permute-start.4
  120.5 4.6 %collective-permute-start.5 = (f32[5,1,1024]{2,1,0:T(1,128)S(1)}, f32[5,1,1024]{2,1,0:T(1,128)S(1)}, u32[]{:S(2)}, u32[]{:S(2)}) collective-permute-start(f32[5,1,1024]{2,1,0:T(1,128)S(1)} %get-tuple-element.67), channel_id=1, source_target_pairs={{0,1},{1,2},{2,3},{4,5},{5,6},{6,7},{8,9},{9,10},{10,11},{12,13},{... | collective-permute-start | bytes 61448 | tf_op jit(solution)/shard_map/ppermute | solution.py:19
  126.6 7.8 %psum.7 = f32[48]{0:T(128)S(1)} all-reduce(f32[48]{0:T(128)S(1)} %broadcast_in_dim.208), channel_id=1, replica_groups=mesh['brick'=128,'span'=4] {'span'}, use_global_device_ids=true, to_apply=%region_9.10 | all-reduce | flops 48 | bytes 384 | tf_op jit(solution)/shard_map/psum | solution.py:199
  135.1 7.8 %all-to-all-start.3 = ((f32[128,1,48]{2,1,0:T(1,128)}), f32[128,1,48]{2,1,0:T(1,128)S(1)}, u32[]{:S(2)}, u32[]{:S(2)}) async-start(f32[128,1,48]{2,1,0:T(1,128)} %broadcast_in_dim.209), calls=%async_computation.3 | async-start | bytes 131072 | tf_op jit(solution)/shard_map/all_to_all | solution.py:201
  143.2 1.3 add_bitcast_fusion
  144.5 10.0 %all-to-all-done.3 = f32[128,1,48]{2,1,0:T(1,128)S(1)} async-done(((f32[128,1,48]{2,1,0:T(1,128)}), f32[128,1,48]{2,1,0:T(1,128)S(1)}, u32[]{:S(2)}, u32[]{:S(2)}) %all-to-all-start.3) | async-done | bytes 24608 | tf_op jit(solution)/shard_map/all_to_all | solution.py:201
  (135 shorter events, 23.0 us)
Async XLA Ops:
  5.9 0.7 copy-start.3
  6.0 1.5 copy-start
  10.2 20.0 %copy-start.4 = (f32[1,1,1024]{2,1,0:T(1,128)S(1)}, f32[1,1,1024]{2,1,0:T(1,128)}, u32[]{:S(2)}) copy-start(f32[1,1,1024]{2,1,0:T(1,128)} %param.19) | copy-start | bytes 12292
  10.2 20.1 %copy-start.5 = (s32[1,1,1024]{2,1,0:T(1,128)S(1)}, s32[1,1,1024]{2,1,0:T(1,128)}, u32[]{:S(2)}) copy-start(s32[1,1,1024]{2,1,0:T(1,128)} %param.18) | copy-start | bytes 12292
  10.2 22.1 %copy-start.1 = (f32[5,5]{1,0:T(8,128)S(1)}, f32[5,5]{1,0:T(8,128)}, u32[]{:S(2)}) copy-start(f32[5,5]{1,0:T(8,128)} %param.11) | copy-start | bytes 304
  10.2 22.1 %copy-start.2 = (f32[5,5]{1,0:T(8,128)S(1)}, f32[5,5]{1,0:T(8,128)}, u32[]{:S(2)}) copy-start(f32[5,5]{1,0:T(8,128)} %param.12) | copy-start | bytes 304
  11.7 31.2 %all-to-all-start = ((f32[128,1,192]{2,1,0:T(1,128)}), f32[128,1,192]{2,1,0:T(1,128)S(1)}, u32[]{:S(2)}, u32[]{:S(2)}) async-start(f32[128,1,192]{2,1,0:T(1,128)} %copy.55), calls=%async_computation | async-start | bytes 262144 | tf_op jit(solution)/shard_map/all_to_all | solution.py:105
  30.3 4.8 %collective-permute-start.6 = (f32[3,1024]{1,0:T(4,128)S(1)}, f32[3,1024]{1,0:T(4,128)S(1)}, u32[]{:S(2)}, u32[]{:S(2)}) collective-permute-start(f32[3,1024]{1,0:T(4,128)S(1)} %pad_maximum_fusion.16), channel_id=1, source_target_pairs={{1,0},{2,1},{3,2},{5,4},{6,5},{7,6},{9,8},{10,9},{11,10},{13,12},{... | collective-permute-start | bytes 36872 | tf_op jit(solution)/shard_map/ppermute | solution.py:175
  47.7 5.6 %collective-permute-start = (f32[5,1,1024]{2,1,0:T(1,128)S(1)}, f32[5,1,1024]{2,1,0:T(1,128)S(1)}, u32[]{:S(2)}, u32[]{:S(2)}) collective-permute-start(f32[5,1,1024]{2,1,0:T(1,128)S(1)} %get-tuple-element.95), channel_id=1, source_target_pairs={{1,0},{2,1},{3,2},{5,4},{6,5},{7,6},{9,8},{10,9},{11,10},{13,12},{... | collective-permute-start | bytes 61448 | tf_op jit(solution)/shard_map/ppermute | solution.py:22
  49.0 4.9 %collective-permute-start.1 = (f32[5,1,1024]{2,1,0:T(1,128)S(1)}, f32[5,1,1024]{2,1,0:T(1,128)S(1)}, u32[]{:S(2)}, u32[]{:S(2)}) collective-permute-start(f32[5,1,1024]{2,1,0:T(1,128)S(1)} %get-tuple-element.94), channel_id=1, source_target_pairs={{0,1},{1,2},{2,3},{4,5},{5,6},{6,7},{8,9},{9,10},{10,11},{12,13},{... | collective-permute-start | bytes 61448 | tf_op jit(solution)/shard_map/ppermute | solution.py:19
  58.9 20.7 %all-to-all-start.1 = ((f32[128,1,160]{2,1,0:T(1,128)}), f32[128,1,160]{2,1,0:T(1,128)S(1)}, u32[]{:S(2)}, u32[]{:S(2)}) async-start(f32[128,1,160]{2,1,0:T(1,128)} %copy.59), calls=%async_computation.1 | async-start | bytes 262144 | tf_op jit(solution)/shard_map/all_to_all | solution.py:105
  83.8 6.2 %collective-permute-start.2 = (f32[5,1,1024]{2,1,0:T(1,128)S(1)}, f32[5,1,1024]{2,1,0:T(1,128)S(1)}, u32[]{:S(2)}, u32[]{:S(2)}) collective-permute-start(f32[5,1,1024]{2,1,0:T(1,128)S(1)} %get-tuple-element.86), channel_id=1, source_target_pairs={{1,0},{2,1},{3,2},{5,4},{6,5},{7,6},{9,8},{10,9},{11,10},{13,12},{... | collective-permute-start | bytes 61448 | tf_op jit(solution)/shard_map/ppermute | solution.py:22
  85.1 5.4 %collective-permute-start.3 = (f32[5,1,1024]{2,1,0:T(1,128)S(1)}, f32[5,1,1024]{2,1,0:T(1,128)S(1)}, u32[]{:S(2)}, u32[]{:S(2)}) collective-permute-start(f32[5,1,1024]{2,1,0:T(1,128)S(1)} %get-tuple-element.85), channel_id=1, source_target_pairs={{0,1},{1,2},{2,3},{4,5},{5,6},{6,7},{8,9},{9,10},{10,11},{12,13},{... | collective-permute-start | bytes 61448 | tf_op jit(solution)/shard_map/ppermute | solution.py:19
  95.6 19.3 %all-to-all-start.2 = ((f32[128,1,160]{2,1,0:T(1,128)}), f32[128,1,160]{2,1,0:T(1,128)S(1)}, u32[]{:S(2)}, u32[]{:S(2)}) async-start(f32[128,1,160]{2,1,0:T(1,128)} %copy.62), calls=%async_computation.2 | async-start | bytes 262144 | tf_op jit(solution)/shard_map/all_to_all | solution.py:105
  119.0 24.1 %collective-permute-start.4 = (f32[5,1,1024]{2,1,0:T(1,128)S(1)}, f32[5,1,1024]{2,1,0:T(1,128)S(1)}, u32[]{:S(2)}, u32[]{:S(2)}) collective-permute-start(f32[5,1,1024]{2,1,0:T(1,128)S(1)} %get-tuple-element.68), channel_id=1, source_target_pairs={{1,0},{2,1},{3,2},{5,4},{6,5},{7,6},{9,8},{10,9},{11,10},{13,12},{... | collective-permute-start | bytes 61448 | tf_op jit(solution)/shard_map/ppermute | solution.py:22
  120.5 22.6 %collective-permute-start.5 = (f32[5,1,1024]{2,1,0:T(1,128)S(1)}, f32[5,1,1024]{2,1,0:T(1,128)S(1)}, u32[]{:S(2)}, u32[]{:S(2)}) collective-permute-start(f32[5,1,1024]{2,1,0:T(1,128)S(1)} %get-tuple-element.67), channel_id=1, source_target_pairs={{0,1},{1,2},{2,3},{4,5},{5,6},{6,7},{8,9},{9,10},{10,11},{12,13},{... | collective-permute-start | bytes 61448 | tf_op jit(solution)/shard_map/ppermute | solution.py:19
  135.1 19.3 %all-to-all-start.3 = ((f32[128,1,48]{2,1,0:T(1,128)}), f32[128,1,48]{2,1,0:T(1,128)S(1)}, u32[]{:S(2)}, u32[]{:S(2)}) async-start(f32[128,1,48]{2,1,0:T(1,128)} %broadcast_in_dim.209), calls=%async_computation.3 | async-start | bytes 131072 | tf_op jit(solution)/shard_map/all_to_all | solution.py:201

commit v2 on v1

--- a/solution.py
+++ b/solution.py
@@ -78,12 +78,28 @@
     row_lo = row_iota == donor_i[None, :]
     row_hi = row_iota == donor_i[None, :] + 1
 
-    def interpolate(field):
-        shifted = jnp.concatenate([field[..., 1:], field[..., :1]], axis=-1)
-        pieces = split_parts(jnp.stack([field, shifted]))
-        picked = lax.dot_general(
-            pieces, col_mat, (((4,), (0,)), ((), ())), preferred_element_type=F32
-        )
+    next_col_mat = (
+        jnp.arange(col_count, dtype=jnp.int32)[:, None] == donor_j[None, :] + 1
+    ).astype(BF16)
+
+    def interpolate(field, select_next=False):
+        if select_next:
+            pieces = split_parts(field)
+            picked = jnp.stack(
+                [
+                    lax.dot_general(
+                        pieces, mat, (((3,), (0,)), ((), ())), preferred_element_type=F32
+                    )
+                    for mat in (col_mat, next_col_mat)
+                ],
+                axis=1,
+            )
+        else:
+            shifted = jnp.concatenate([field[..., 1:], field[..., :1]], axis=-1)
+            pieces = split_parts(jnp.stack([field, shifted]))
+            picked = lax.dot_general(
+                pieces, col_mat, (((4,), (0,)), ((), ())), preferred_element_type=F32
+            )
         picked = join_parts(picked)
         at_lo = jnp.sum(jnp.where(row_lo[None, None], picked, 0.0), axis=2)
         at_hi = jnp.sum(jnp.where(row_hi[None, None], picked, 0.0), axis=2)
@@ -107,7 +123,7 @@
 
     local_state = state[:, 0]
 
-    first_interp = interpolate(local_state)
+    first_interp = interpolate(local_state, select_next=True)
     target_code = (target_cell + 1).astype(F32)
     received = exchange(jnp.concatenate([first_interp, target_code[None]], axis=0))
     slot_count = peer_count * capacity

time: 156 us -> 155 us (level)
  local copies, waits for them, and re-layouts: 10.9 us -> 7.43 us
  matrix products: 19.4 us -> 22.2 us
    dot_general x0 -> x2, matrix products: none -> 4.76 us  [interpolate(): lax.dot_general(pieces, mat, (((3,), (0,)), ((), ())), preferred_element_...]
    dot_general x3 -> x2, matrix products: 5.72 us -> 3.81 us  [interpolate(): lax.dot_general(pieces, col_mat, (((4,), (0,)), ((), ())), preferred_elem...]
    slice x6 -> x4, local copies, waits for them, and re-layouts: 2.2 us -> 0.3 us  [interpolate(): shifted = jnp.concatenate([field[..., 1:], field[..., :1]], axis=-1)]
where the time goes in v2:
time: 155 us
  starting transfers between devices  59 us (38%)
  waiting for transfers between devices  47 us (30%)
  matrix products  22.2 us (14%)
  other arithmetic  9.29 us (6%)
  blocking collectives  7.82 us (5%)
  local copies, waits for them, and re-layouts  7.43 us (5%)
  between operations  2.11 us (1%)
    all_to_all x3, waiting for transfers between devices, exchange(): moved = lax.all_to_all(flat, 'brick', 0, 0, tiled=True)  33.3 us
    all_to_all x3, starting transfers between devices, exchange(): moved = lax.all_to_all(flat, 'brick', 0, 0, tiled=True)  32.8 us
    ppermute x3, starting transfers between devices, with_halo(): lax.ppermute(lax.slice_in_dim(block, block.shape[dim] - width, None, axis...  13.1 us
    dot_general x3, matrix products, to_cells(): lax.dot_general(spread, cell_mat, (((3,), (0,)), ((), ())), preferred_ele...  10.4 us
    all_to_all x1, waiting for transfers between devices, shards(): gathered = lax.all_to_all(copies, 'brick', 0, 0, tiled=True)  9.97 us
    psum x1, blocking collectives, shards(): span_loads = lax.psum(partial_loads, 'span')  7.82 us
    all_to_all x1, starting transfers between devices, shards(): gathered = lax.all_to_all(copies, 'brick', 0, 0, tiled=True)  7.72 us
    dot_general x2, matrix products, interpolate(): lax.dot_general(pieces, mat, (((3,), (0,)), ((), ())), preferred_element_...  4.76 us
  transfers between devices with their start and end apart: 11, of which 7 were waited for; matrix products, arithmetic and copies ran while one was open for 3% of the time, Pallas kernels for 0%

profile of v2, /device:TPU:1, one launch (start us, length us, event | category | flops | bytes accessed | tf_op | source)
XLA Modules:
  0.0 154.8 jit_solution(14007285667938779714)
XLA Ops:
  2.4 1.8 %fusion.25 = f32[2,1,5,16,2048]{4,3,2,0,1:T(8,128)S(1)} fusion(s32[2048]{0:T(1024)S(1)} %get-tuple-element.120, bf16[1,5,16,1024]{3,2,1,0:T(8,128)(2,1)S(1)} %get-tuple-element.95, bf16[1,5,16,1024]{3,2,1,0:T(8,128)(2,1)S(1)} %get-tuple-element.94), kind=kOutput, calls=%fused_computation.23 | convolution fusion | flops 673349632 | bytes 1646592 | tf_op jit(solution)/shard_map/dot_general | solution.py:90
  4.3 2.9 %fusion.28 = f32[2,1,5,16,2048]{4,3,2,0,1:T(8,128)} fusion(s32[2048]{0:T(1024)S(1)} %get-tuple-element.119, bf16[1,5,16,1024]{3,2,1,0:T(8,128)(2,1)S(1)} %get-tuple-element.95, bf16[1,5,16,1024]{3,2,1,0:T(8,128)(2,1)S(1)} %get-tuple-element.94), kind=kOutput, calls=%fused_computation.24 | convolution fusion | flops 673349632 | bytes 1646592 | tf_op jit(solution)/shard_map/dot_general | solution.py:90
  11.3 18.4 %all-to-all-start = ((f32[128,1,192]{2,1,0:T(1,128)}), f32[128,1,192]{2,1,0:T(1,128)S(1)}, u32[]{:S(2)}, u32[]{:S(2)}) async-start(f32[128,1,192]{2,1,0:T(1,128)} %copy.55), calls=%async_computation | async-start | bytes 262144 | tf_op jit(solution)/shard_map/all_to_all | solution.py:121
  30.0 1.5 collective-permute-start.6
  32.4 2.3 %collective-permute-done.6 = f32[3,1024]{1,0:T(4,128)S(1)} collective-permute-done((f32[3,1024]{1,0:T(4,128)S(1)}, f32[3,1024]{1,0:T(4,128)S(1)}, u32[]{:S(2)}, u32[]{:S(2)}) %collective-permute-start.6) | collective-permute-done | bytes 12320 | tf_op jit(solution)/shard_map/ppermute | solution.py:191
  34.8 7.7 %all-to-all-done = f32[128,1,192]{2,1,0:T(1,128)S(1)} async-done(((f32[128,1,192]{2,1,0:T(1,128)}), f32[128,1,192]{2,1,0:T(1,128)S(1)}, u32[]{:S(2)}, u32[]{:S(2)}) %all-to-all-start) | async-done | bytes 98336 | tf_op jit(solution)/shard_map/all_to_all | solution.py:121
  43.5 3.6 %fusion.5 = f32[2,6,16,1024]{3,2,1,0:T(8,128)S(1)} fusion(s32[4096]{0:T(1024)S(1)} %get-tuple-element.111, bf16[2,1,16,4096]{3,2,1,0:T(8,128)(2,1)S(1)} %broadcast_in_dim.201, bf16[2,5,16,4096]{3,2,1,0:T(8,128)(2,1)S(1)} %broadcast_select_fusion), kind=kOutput, calls=%fused_computation.4 | convolution fusion | flops 1615593472 | bytes 2375680 | tf_op jit(solution)/shard_map/dot_general | solution.py:147
  47.4 1.3 collective-permute-start
  48.7 4.0 %collective-permute-start.1 = (f32[5,1,1024]{2,1,0:T(1,128)S(1)}, f32[5,1,1024]{2,1,0:T(1,128)S(1)}, u32[]{:S(2)}, u32[]{:S(2)}) collective-permute-start(f32[5,1,1024]{2,1,0:T(1,128)S(1)} %get-tuple-element.92), channel_id=1, source_target_pairs={{0,1},{1,2},{2,3},{4,5},{5,6},{6,7},{8,9},{9,10},{10,11},{12,13},{... | collective-permute-start | bytes 61448 | tf_op jit(solution)/shard_map/ppermute | solution.py:19
  54.5 1.9 %fusion.14 = f32[2,2,5,16,2048]{4,3,2,1,0:T(8,128)S(1)} fusion(s32[2048]{0:T(1024)S(1)} %get-tuple-element.120, bf16[1,2,5,16,1024]{4,3,2,1,0:T(8,128)(2,1)S(1)} %get-tuple-element.55, bf16[1,2,5,16,1024]{4,3,2,1,0:T(8,128)(2,1)S(1)} %get-tuple-element.54), kind=kOutput, calls=%fused_computation.13 | convolution fusion | flops 1344602112 | bytes 3284992 | tf_op jit(solution)/shard_map/dot_general | solution.py:100
  58.5 8.0 %all-to-all-start.1 = ((f32[128,1,160]{2,1,0:T(1,128)}), f32[128,1,160]{2,1,0:T(1,128)S(1)}, u32[]{:S(2)}, u32[]{:S(2)}) async-start(f32[128,1,160]{2,1,0:T(1,128)} %copy.59), calls=%async_computation.1 | async-start | bytes 262144 | tf_op jit(solution)/shard_map/all_to_all | solution.py:121
  66.5 12.7 %all-to-all-done.1 = f32[128,1,160]{2,1,0:T(1,128)S(1)} async-done(((f32[128,1,160]{2,1,0:T(1,128)}), f32[128,1,160]{2,1,0:T(1,128)S(1)}, u32[]{:S(2)}, u32[]{:S(2)}) %all-to-all-start.1) | async-done | bytes 81952 | tf_op jit(solution)/shard_map/all_to_all | solution.py:121
  79.8 3.4 %fusion.3 = f32[2,5,16,1024]{3,2,1,0:T(8,128)S(1)} fusion(s32[4096]{0:T(1024)S(1)} %get-tuple-element.111, pred[16,4096]{1,0:T(8,128)(4,1)S(1)} %get-tuple-element.108, bf16[2,5,4096]{2,1,0:T(8,128)(2,1)S(1)} %pad_maximum_fusion.13), kind=kOutput, calls=%fused_computation.3 | convolution fusion | flops 1347026944 | bytes 819200 | tf_op jit(solution)/shard_map/dot_general | solution.py:147
  83.4 1.3 collective-permute-start.2
  84.7 4.6 %collective-permute-start.3 = (f32[5,1,1024]{2,1,0:T(1,128)S(1)}, f32[5,1,1024]{2,1,0:T(1,128)S(1)}, u32[]{:S(2)}, u32[]{:S(2)}) collective-permute-start(f32[5,1,1024]{2,1,0:T(1,128)S(1)} %get-tuple-element.83), channel_id=1, source_target_pairs={{0,1},{1,2},{2,3},{4,5},{5,6},{6,7},{8,9},{9,10},{10,11},{12,13},{... | collective-permute-start | bytes 61448 | tf_op jit(solution)/shard_map/ppermute | solution.py:19
  91.2 1.9 %fusion.12 = f32[2,2,5,16,2048]{4,3,2,1,0:T(8,128)S(1)} fusion(s32[2048]{0:T(1024)S(1)} %get-tuple-element.120, bf16[1,2,5,16,1024]{4,3,2,1,0:T(8,128)(2,1)S(1)} %get-tuple-element.48, bf16[1,2,5,16,1024]{4,3,2,1,0:T(8,128)(2,1)S(1)} %get-tuple-element.47), kind=kOutput, calls=%fused_computation.12 | convolution fusion | flops 1344602112 | bytes 3284992 | tf_op jit(solution)/shard_map/dot_general | solution.py:100
  95.2 6.4 %all-to-all-start.2 = ((f32[128,1,160]{2,1,0:T(1,128)}), f32[128,1,160]{2,1,0:T(1,128)S(1)}, u32[]{:S(2)}, u32[]{:S(2)}) async-start(f32[128,1,160]{2,1,0:T(1,128)} %copy.62), calls=%async_computation.2 | async-start | bytes 262144 | tf_op jit(solution)/shard_map/all_to_all | solution.py:121
  101.7 12.8 %all-to-all-done.2 = f32[128,1,160]{2,1,0:T(1,128)S(1)} async-done(((f32[128,1,160]{2,1,0:T(1,128)}), f32[128,1,160]{2,1,0:T(1,128)S(1)}, u32[]{:S(2)}, u32[]{:S(2)}) %all-to-all-start.2) | async-done | bytes 81952 | tf_op jit(solution)/shard_map/all_to_all | solution.py:121
  115.0 3.4 %fusion.1 = f32[2,5,16,1024]{3,2,1,0:T(8,128)S(1)} fusion(s32[4096]{0:T(1024)S(1)} %get-tuple-element.111, pred[16,4096]{1,0:T(8,128)(4,1)S(1)} %get-tuple-element.108, bf16[2,5,4096]{2,1,0:T(8,128)(2,1)S(1)} %pad_maximum_fusion.14), kind=kOutput, calls=%fused_computation.2 | convolution fusion | flops 1347026944 | bytes 819200 | tf_op jit(solution)/shard_map/dot_general | solution.py:147
  118.6 1.3 collective-permute-start.4
  120.1 4.6 %collective-permute-start.5 = (f32[5,1,1024]{2,1,0:T(1,128)S(1)}, f32[5,1,1024]{2,1,0:T(1,128)S(1)}, u32[]{:S(2)}, u32[]{:S(2)}) collective-permute-start(f32[5,1,1024]{2,1,0:T(1,128)S(1)} %get-tuple-element.65), channel_id=1, source_target_pairs={{0,1},{1,2},{2,3},{4,5},{5,6},{6,7},{8,9},{9,10},{10,11},{12,13},{... | collective-permute-start | bytes 61448 | tf_op jit(solution)/shard_map/ppermute | solution.py:19
  126.3 7.8 %psum.7 = f32[48]{0:T(128)S(1)} all-reduce(f32[48]{0:T(128)S(1)} %broadcast_in_dim.210), channel_id=1, replica_groups=mesh['brick'=128,'span'=4] {'span'}, use_global_device_ids=true, to_apply=%region_9.10 | all-reduce | flops 48 | bytes 384 | tf_op jit(solution)/shard_map/psum | solution.py:215
  134.7 7.7 %all-to-all-start.3 = ((f32[128,1,48]{2,1,0:T(1,128)}), f32[128,1,48]{2,1,0:T(1,128)S(1)}, u32[]{:S(2)}, u32[]{:S(2)}) async-start(f32[128,1,48]{2,1,0:T(1,128)} %broadcast_in_dim.211), calls=%async_computation.3 | async-start | bytes 131072 | tf_op jit(solution)/shard_map/all_to_all | solution.py:217
  144.1 10.0 %all-to-all-done.3 = f32[128,1,48]{2,1,0:T(1,128)S(1)} async-done(((f32[128,1,48]{2,1,0:T(1,128)}), f32[128,1,48]{2,1,0:T(1,128)S(1)}, u32[]{:S(2)}, u32[]{:S(2)}) %all-to-all-start.3) | async-done | bytes 24608 | tf_op jit(solution)/shard_map/all_to_all | solution.py:217
  (139 shorter events, 21.4 us)
Async XLA Ops:
  4.2 3.0 %copy-start.5 = (f32[2,1,1,2048]{3,2,1,0:T(1,128)S(1)}, f32[2,1,1,2048]{3,2,1,0:T(1,128)}, u32[]{:S(2)}) copy-start(f32[2,1,1,2048]{3,2,1,0:T(1,128)} %param.17) | copy-start | bytes 49156
  4.2 2.9 %copy-start.6 = (s32[1,1,2048]{2,1,0:T(1,128)S(1)}, s32[1,1,2048]{2,1,0:T(1,128)}, u32[]{:S(2)}) copy-start(s32[1,1,2048]{2,1,0:T(1,128)} %param.16) | copy-start | bytes 24580
  4.2 3.0 %copy-start.4 = (s32[1,1,2048]{2,1,0:T(1,128)S(1)}, s32[1,1,2048]{2,1,0:T(1,128)}, u32[]{:S(2)}) copy-start(s32[1,1,2048]{2,1,0:T(1,128)} %param.14) | copy-start | bytes 24580
  7.8 1.3 copy-start
  9.8 20.0 %copy-start.7 = (f32[1,1,1024]{2,1,0:T(1,128)S(1)}, f32[1,1,1024]{2,1,0:T(1,128)}, u32[]{:S(2)}) copy-start(f32[1,1,1024]{2,1,0:T(1,128)} %param.19) | copy-start | bytes 12292
  9.8 20.1 %copy-start.8 = (s32[1,1,1024]{2,1,0:T(1,128)S(1)}, s32[1,1,1024]{2,1,0:T(1,128)}, u32[]{:S(2)}) copy-start(s32[1,1,1024]{2,1,0:T(1,128)} %param.18) | copy-start | bytes 12292
  9.8 22.3 %copy-start.2 = (f32[5,5]{1,0:T(8,128)S(1)}, f32[5,5]{1,0:T(8,128)}, u32[]{:S(2)}) copy-start(f32[5,5]{1,0:T(8,128)} %param.11) | copy-start | bytes 304
  9.8 22.3 %copy-start.3 = (f32[5,5]{1,0:T(8,128)S(1)}, f32[5,5]{1,0:T(8,128)}, u32[]{:S(2)}) copy-start(f32[5,5]{1,0:T(8,128)} %param.12) | copy-start | bytes 304
  11.3 31.2 %all-to-all-start = ((f32[128,1,192]{2,1,0:T(1,128)}), f32[128,1,192]{2,1,0:T(1,128)S(1)}, u32[]{:S(2)}, u32[]{:S(2)}) async-start(f32[128,1,192]{2,1,0:T(1,128)} %copy.55), calls=%async_computation | async-start | bytes 262144 | tf_op jit(solution)/shard_map/all_to_all | solution.py:121
  30.0 4.8 %collective-permute-start.6 = (f32[3,1024]{1,0:T(4,128)S(1)}, f32[3,1024]{1,0:T(4,128)S(1)}, u32[]{:S(2)}, u32[]{:S(2)}) collective-permute-start(f32[3,1024]{1,0:T(4,128)S(1)} %pad_maximum_fusion.19), channel_id=1, source_target_pairs={{1,0},{2,1},{3,2},{5,4},{6,5},{7,6},{9,8},{10,9},{11,10},{13,12},{... | collective-permute-start | bytes 36872 | tf_op jit(solution)/shard_map/ppermute | solution.py:191
  43.5 3.7 %copy-start.1 = (f32[5,1,16,1024]{3,2,1,0:T(8,128)S(1)}, f32[5,1,16,1024]{3,2,1,0:T(8,128)}, u32[]{:S(2)}) copy-start(f32[5,1,16,1024]{3,2,1,0:T(8,128)} %param.10) | copy-start | bytes 983044
  47.4 5.5 %collective-permute-start = (f32[5,1,1024]{2,1,0:T(1,128)S(1)}, f32[5,1,1024]{2,1,0:T(1,128)S(1)}, u32[]{:S(2)}, u32[]{:S(2)}) collective-permute-start(f32[5,1,1024]{2,1,0:T(1,128)S(1)} %get-tuple-element.93), channel_id=1, source_target_pairs={{1,0},{2,1},{3,2},{5,4},{6,5},{7,6},{9,8},{10,9},{11,10},{13,12},{... | collective-permute-start | bytes 61448 | tf_op jit(solution)/shard_map/ppermute | solution.py:22
  48.7 4.9 %collective-permute-start.1 = (f32[5,1,1024]{2,1,0:T(1,128)S(1)}, f32[5,1,1024]{2,1,0:T(1,128)S(1)}, u32[]{:S(2)}, u32[]{:S(2)}) collective-permute-start(f32[5,1,1024]{2,1,0:T(1,128)S(1)} %get-tuple-element.92), channel_id=1, source_target_pairs={{0,1},{1,2},{2,3},{4,5},{5,6},{6,7},{8,9},{9,10},{10,11},{12,13},{... | collective-permute-start | bytes 61448 | tf_op jit(solution)/shard_map/ppermute | solution.py:19
  58.5 20.7 %all-to-all-start.1 = ((f32[128,1,160]{2,1,0:T(1,128)}), f32[128,1,160]{2,1,0:T(1,128)S(1)}, u32[]{:S(2)}, u32[]{:S(2)}) async-start(f32[128,1,160]{2,1,0:T(1,128)} %copy.59), calls=%async_computation.1 | async-start | bytes 262144 | tf_op jit(solution)/shard_map/all_to_all | solution.py:121
  83.4 6.0 %collective-permute-start.2 = (f32[5,1,1024]{2,1,0:T(1,128)S(1)}, f32[5,1,1024]{2,1,0:T(1,128)S(1)}, u32[]{:S(2)}, u32[]{:S(2)}) collective-permute-start(f32[5,1,1024]{2,1,0:T(1,128)S(1)} %get-tuple-element.84), channel_id=1, source_target_pairs={{1,0},{2,1},{3,2},{5,4},{6,5},{7,6},{9,8},{10,9},{11,10},{13,12},{... | collective-permute-start | bytes 61448 | tf_op jit(solution)/shard_map/ppermute | solution.py:22
  84.7 5.5 %collective-permute-start.3 = (f32[5,1,1024]{2,1,0:T(1,128)S(1)}, f32[5,1,1024]{2,1,0:T(1,128)S(1)}, u32[]{:S(2)}, u32[]{:S(2)}) collective-permute-start(f32[5,1,1024]{2,1,0:T(1,128)S(1)} %get-tuple-element.83), channel_id=1, source_target_pairs={{0,1},{1,2},{2,3},{4,5},{5,6},{6,7},{8,9},{9,10},{10,11},{12,13},{... | collective-permute-start | bytes 61448 | tf_op jit(solution)/shard_map/ppermute | solution.py:19
  95.2 19.3 %all-to-all-start.2 = ((f32[128,1,160]{2,1,0:T(1,128)}), f32[128,1,160]{2,1,0:T(1,128)S(1)}, u32[]{:S(2)}, u32[]{:S(2)}) async-start(f32[128,1,160]{2,1,0:T(1,128)} %copy.62), calls=%async_computation.2 | async-start | bytes 262144 | tf_op jit(solution)/shard_map/all_to_all | solution.py:121
  118.6 24.0 %collective-permute-start.4 = (f32[5,1,1024]{2,1,0:T(1,128)S(1)}, f32[5,1,1024]{2,1,0:T(1,128)S(1)}, u32[]{:S(2)}, u32[]{:S(2)}) collective-permute-start(f32[5,1,1024]{2,1,0:T(1,128)S(1)} %get-tuple-element.66), channel_id=1, source_target_pairs={{1,0},{2,1},{3,2},{5,4},{6,5},{7,6},{9,8},{10,9},{11,10},{13,12},{... | collective-permute-start | bytes 61448 | tf_op jit(solution)/shard_map/ppermute | solution.py:22
  120.1 22.5 %collective-permute-start.5 = (f32[5,1,1024]{2,1,0:T(1,128)S(1)}, f32[5,1,1024]{2,1,0:T(1,128)S(1)}, u32[]{:S(2)}, u32[]{:S(2)}) collective-permute-start(f32[5,1,1024]{2,1,0:T(1,128)S(1)} %get-tuple-element.65), channel_id=1, source_target_pairs={{0,1},{1,2},{2,3},{4,5},{5,6},{6,7},{8,9},{9,10},{10,11},{12,13},{... | collective-permute-start | bytes 61448 | tf_op jit(solution)/shard_map/ppermute | solution.py:19
  134.7 19.3 %all-to-all-start.3 = ((f32[128,1,48]{2,1,0:T(1,128)}), f32[128,1,48]{2,1,0:T(1,128)S(1)}, u32[]{:S(2)}, u32[]{:S(2)}) async-start(f32[128,1,48]{2,1,0:T(1,128)} %broadcast_in_dim.211), calls=%async_computation.3 | async-start | bytes 131072 | tf_op jit(solution)/shard_map/all_to_all | solution.py:217
